TPU v7x, 128 devices: a whole 4x4x4 slice. The times are simulated.
128 devices in a mesh: path: 16 (over x, y_lo, core), trade: 8 (over y_hi, z).
Axes of the slice: x: 4, y: 4 (y_hi: 2, y_lo: 2; y = y_hi * 2 + y_lo), z: 4, core: 2. Of those that a mesh axis runs over, the one named last changes fastest.
Arguments:
- factors: bfloat16 [65536, 256], P('path'), may hold values from -6 to 6
- exposures: bfloat16 [16384, 256], P('trade'), may hold values from -0.375 to 0.375
- strikes: float32 [16384], P('trade'), may hold values from -1 to 1
- notionals: float32 [16384], P('trade'), may hold values from -0.09375 to 0.09375
- w_first: float32 [256, 1024], replicated, may hold values from -0.375 to 0.375
- b_first: float32 [1024], replicated, may hold values from -3 to 3
- w_second: float32 [1024, 1024], replicated, may hold values from -0.1875 to 0.1875
- b_second: float32 [1024], replicated, may hold values from -3 to 3
- w_out: float32 [1024], replicated, may hold values from -0.1875 to 0.1875
- b_out: float32 [1], replicated, may hold values from -3 to 3
Outputs:
- grad_w_first: float32 [256, 1024], replicated
- grad_b_first: float32 [1024], replicated
- grad_w_second: float32 [1024, 1024], replicated
- grad_b_second: float32 [1024], replicated
- grad_w_out: float32 [1024], replicated
- grad_b_out: float32 [1], replicated
All inputs are finite; a program needn't handle non-finite values.
Results may differ from a plain program's by a relative error of at most 0.0003.
Values sent between devices are 32-bit elements; how exact they have to be, the bound alone decides.
No kernel may reach another device: no remote copies, remote signals or barrier semaphores. Data moves between devices by JAX's collectives and lax.ppermute only.
A program may use at most 128 MiB of HBM per device.

v0:
```python
import jax
import jax.numpy as jnp
from jax import lax
from jax.sharding import PartitionSpec as P
from jax.experimental import pallas as pl
from jax.experimental.pallas import tpu as pltpu


def twin_loss(params, inputs, value, differential, scale):
    w_first, b_first, w_second, b_second, w_out, b_out = params
    highest = lax.Precision.HIGH
    act_one = jnp.dot(inputs, w_first, precision=highest) + b_first
    hid_one = jax.nn.softplus(act_one)
    act_two = jnp.dot(hid_one, w_second, precision=highest) + b_second
    hid_two = jax.nn.softplus(act_two)
    predicted = jnp.dot(hid_two, w_out, precision=highest) + b_out[0]
    back_two = w_out * jax.nn.sigmoid(act_two)
    back_one = jnp.dot(back_two, w_second.T, precision=highest) * jax.nn.sigmoid(act_one)
    slope = jnp.dot(back_one, w_first.T, precision=highest)
    miss_value = predicted - value
    miss_slope = slope - differential
    return (jnp.sum(miss_value * miss_value) + jnp.sum(miss_slope * miss_slope)) * scale


ROW_CHUNK = 16
LANE_CHUNK = 256


def price_kernel(f_ref, e_ref, s_ref, n_ref, d_ref, v_ref, m_scr, w_scr):
    m_scr[...] = lax.dot_general(
        f_ref[...], e_ref[...], (((1,), (1,)), ((), ())), preferred_element_type=jnp.float32
    )
    tile, trades = m_scr.shape

    def rows(i, carry):
        r = pl.multiple_of(i * ROW_CHUNK, ROW_CHUNK)
        acc = jnp.zeros((ROW_CHUNK, 128), jnp.float32)
        for c in range(trades // LANE_CHUNK):
            cs = slice(c * LANE_CHUNK, (c + 1) * LANE_CHUNK)
            m = m_scr[pl.ds(r, ROW_CHUNK), cs] - s_ref[:, cs]
            notional = n_ref[:, cs]
            e = jnp.exp(-jnp.abs(m))
            soft = jnp.maximum(m, 0.0) + jnp.log1p(e)
            rcp = 1.0 / (1.0 + e)
            sig = jnp.where(m >= 0.0, rcp, e * rcp)
            w_scr[pl.ds(r, ROW_CHUNK), cs] = (sig * notional).astype(jnp.bfloat16)
            t = soft * notional
            for g in range(LANE_CHUNK // 128):
                acc = acc + t[:, g * 128 : (g + 1) * 128]
        v_ref[pl.ds(r, ROW_CHUNK), :] = acc
        return carry

    lax.fori_loop(0, tile // ROW_CHUNK, rows, 0)
    d_ref[...] = jnp.dot(w_scr[...], e_ref[...], preferred_element_type=jnp.float32)


def price(factors, exposures, strikes, notionals, tile=256):
    paths, width = factors.shape
    trades = exposures.shape[0]
    return pl.pallas_call(
        price_kernel,
        grid=(paths // tile,),
        in_specs=[
            pl.BlockSpec((tile, width), lambda i: (i, 0)),
            pl.BlockSpec((trades, width), lambda i: (0, 0)),
            pl.BlockSpec((1, trades), lambda i: (0, 0)),
            pl.BlockSpec((1, trades), lambda i: (0, 0)),
        ],
        out_specs=[
            pl.BlockSpec((tile, width), lambda i: (i, 0)),
            pl.BlockSpec((tile, 128), lambda i: (i, 0)),
        ],
        out_shape=[
            jax.ShapeDtypeStruct((paths, width), jnp.float32),
            jax.ShapeDtypeStruct((paths, 128), jnp.float32),
        ],
        scratch_shapes=[
            pltpu.VMEM((tile, trades), jnp.float32),
            pltpu.VMEM((tile, trades), jnp.bfloat16),
        ],
    )(factors, exposures, strikes.reshape(1, trades), notionals.reshape(1, trades))


def body(
    factors, exposures, strikes, notionals, w_first, b_first, w_second, b_second, w_out, b_out
):
    paths, width = factors.shape
    with jax.named_scope("price_trades"):
        differential, value_parts = price(factors, exposures, strikes, notionals)
    value = jnp.sum(value_parts, axis=1)
    groups = lax.axis_size("trade")
    own_rows = paths // groups
    first_row = lax.axis_index("trade") * own_rows
    value_rows = -(-own_rows // width)
    value_pad = jnp.pad(value.reshape(groups, own_rows), ((0, 0), (0, value_rows * width - own_rows)))
    packed = jnp.concatenate(
        [differential.reshape(groups, own_rows, width), value_pad.reshape(groups, value_rows, width)],
        axis=1,
    )
    mine = lax.psum_scatter(packed, "trade", scatter_dimension=0, tiled=False)
    my_diff = mine[:own_rows]
    my_value = mine[own_rows:].reshape(-1)[:own_rows]
    my_inputs = lax.dynamic_slice_in_dim(factors, first_row, own_rows, 0).astype(jnp.float32)
    scale = 1.0 / jnp.sqrt(jnp.float32(paths * lax.axis_size("path")))
    params = (w_first, b_first, w_second, b_second, w_out, b_out)
    grads = jax.grad(twin_loss)(params, my_inputs, my_value, my_diff, scale)
    hidden = w_second.shape[0]
    small = jnp.stack([grads[1], grads[3], grads[4], jnp.pad(grads[5], (0, hidden - 1))])
    head = jnp.concatenate([grads[0], small], axis=0)
    head, g2 = lax.psum((head, grads[2]), ("path", "trade"))
    n0 = w_first.shape[0]
    g0 = head[:n0]
    tail = head[n0:]
    return (g0, tail[0], g2, tail[1], tail[2], tail[3, :1])

def solution(mesh):
    in_specs = (
        P("path", None),
        P("trade", None),
        P("trade"),
        P("trade"),
        P(),
        P(),
        P(),
        P(),
        P(),
        P(),
    )
    out_specs = (P(), P(), P(), P(), P(), P())
    return jax.shard_map(body, mesh=mesh, in_specs=in_specs, out_specs=out_specs, check_vma=False)
```

profile of v0, /device:TPU:1, one launch (start us, length us, event | category | flops | bytes accessed | tf_op | source)
XLA Modules:
  0.0 364.3 jit_solution(4031827188441739529)
XLA Ops:
  7.2 0.0 copy-start
  7.2 0.0 reduce-scatter.2.cloned.1.call-start
  7.2 53.2 %price_trades.1 = (f32[4096,256]{1,0:T(8,128)}, f32[4096,128]{1,0:T(8,128)}) custom-call(bf16[4096,256]{1,0:T(8,128)(2,1)} %f_ref.1, bf16[2048,256]{1,0:T(8,128)(2,1)} %e_ref.1, f32[1,2048]{1,0:T(1,128)} %bitcast.42, f32[1,2048]{1,0:T(1,128)} %bitcast.43), custom_call_target="tpu_custom_call" | custom-call | tf_op jit(solution)/shard_map/price_trades/pallas_call | solution.py:60
  60.4 2.2 reduce_sum.43
  62.6 4.5 %pad_maximum_fusion = f32[8,514,256]{2,1,0:T(8,128)} fusion(f32[8,2,256]{2,1,0:T(2,128)S(1)} %reshape.51, f32[8,512,256]{2,1,0:T(8,128)} %bitcast.39), kind=kLoop, calls=%fused_computation.6 | loop fusion | flops 1052672 | bytes 8421376 | tf_op jit(solution)/shard_map/concatenate | solution.py:96
  67.2 0.0 reduce-scatter.2.cloned.1.call-update
  67.2 0.0 all-reduce.4.cloned.1.call-start
  67.9 1.7 fusion.28
  69.7 7.6 %fusion.24 = f32[512,1024]{1,0:T(8,128)S(1)} fusion(f32[1024,1024]{1,0:T(8,128)} %param.17, f32[512,1024]{1,0:T(8,128)S(1)} %fusion.28, f32[1024]{0:T(1024)S(1)} %copy-done.1), kind=kOutput, calls=%fused_computation.39 | convolution fusion | flops 3224895488 | bytes 8392704 | tf_op jit(solution)/shard_map/jvp()/dot_general | solution.py:14
  77.3 2.0 fusion.26
  79.3 1.0 copy-done.2
  80.3 5.2 %fusion.12 = f32[512,1024]{1,0:T(8,128)} fusion(f32[1024,1024]{1,0:T(8,128)S(1)} %copy-done.2, f32[1024]{0:T(1024)S(1)} %copy-done.4, f32[512,1024]{1,0:T(8,128)S(1)} %fusion.24, f32[1024]{0:T(1024)S(1)} %copy-done.5), kind=kOutput, calls=%fused_computation.25 | convolution fusion | flops 3223846912 | bytes 8396800 | tf_op jit(solution)/shard_map/jvp()/dot_general | solution.py:18
  85.4 69.6 %reduce-scatter.2.cloned.1.call-done = f32[1,514,256]{2,1,0:T(8,128)} async-done(((f32[8,514,256]{2,1,0:T(8,128)}), f32[1,514,256]{2,1,0:T(8,128)}) %reduce-scatter.2.cloned.1.call-update) | async-done | bytes 526352 | tf_op jit(solution)/shard_map/reduce_scatter | solution.py:100
  155.0 3.2 fusion.15
  158.3 1.5 fusion.21
  159.8 1.0 fusion.41
  160.8 0.7 slice_bitcast_fusion.1
  161.5 4.5 %fusion.10 = f32[1024,1024]{1,0:T(8,128)S(1)} fusion(f32[1024]{0:T(1024)S(1)} %copy-done.4, f32[512,1024]{1,0:T(8,128)S(1)} %fusion.41, f32[512,1024]{1,0:T(8,128)S(1)} %copy-done.7, f32[1024]{0:T(1024)S(1)} %copy-done.5, f32[512,1024]{1,0:T(8,128)S(1)} %fusion.28, f32[1024]{0:T(1024)S(1)} %copy-done.1), kind=kOutput, calls=%fused_computation.23 | convolution fusion | flops 3226468352 | bytes 10498048 | tf_op jit(solution)/shard_map/transpose(jvp())/dot_general | solution.py:18
  166.0 0.6 fusion.36
  166.6 5.7 %fusion.37 = (f32[1024]{0:T(1024)S(1)}, f32[512,1024]{1,0:T(8,128)S(1)}, f32[1024]{0:T(1024)S(1)}) fusion(f32[512]{0:T(512)S(1)} %get-tuple-element.21, f32[512,1024]{1,0:T(8,128)S(1)} %copy-done.7, f32[1024]{0:T(1024)S(1)} %copy-done.5, f32[1024]{0:T(1024)S(1)} %copy-done.4, f32[1024,1024]{1,0:T(8,128)S(1)} %copy-done.3, f32[512,1024]{1,0:T(8,128)S(1)} %fusion.41, ...), kind=kOutput, calls=%fused_computation.55 | convolution fusion | flops 3236952064 | bytes 12605440 | tf_op jit(solution)/shard_map/transpose(jvp())/dot_general | solution.py:18
  172.4 5.3 %fusion.40 = (f32[1024]{0:T(1024)S(1)}, f32[512,1024]{1,0:T(8,128)S(1)}) fusion(f32[512,1024]{1,0:T(8,128)S(1)} %get-tuple-element.23, f32[1024,1024]{1,0:T(8,128)S(1)} %copy-done.3, f32[512,1024]{1,0:T(8,128)S(1)} %fusion.28, f32[1024]{0:T(1024)S(1)} %copy-done.1, f32[512,1024]{1,0:T(8,128)S(1)} %copy-done.8, f32[512,1024]{1,0:T(8,128)S(1)} %fusion.41), kind=kOutput, calls=%fused_computation.57 | convolution fusion | flops 3232758784 | bytes 14688256 | tf_op jit(solution)/shard_map/transpose(jvp())/dot_general | solution.py:14
  177.7 1.9 fusion.25
  179.6 0.7 pad.4
  180.3 6.8 %convolution_add_fusion = f32[1024,1024]{1,0:T(8,128)} fusion(f32[1024,1024]{1,0:T(8,128)S(1)} %fusion.10, f32[512,1024]{1,0:T(8,128)S(1)} %get-tuple-element.23, f32[512,1024]{1,0:T(8,128)S(1)} %fusion.28, f32[1024]{0:T(1024)S(1)} %copy-done.1), kind=kOutput, calls=%fused_computation.9 | convolution fusion | flops 3225944064 | bytes 12587008 | tf_op jit(solution)/shard_map/transpose(jvp())/dot_general | solution.py:14
  187.1 1.8 convolution_add_fusion.1
  188.8 2.2 concatenate.7
  191.1 0.0 all-reduce.4.cloned.1.call-update
  191.1 156.6 %all-reduce.4.cloned.1.call-done = (f32[260,1024]{1,0:T(8,128)}, f32[1024,1024]{1,0:T(8,128)}) async-done(((f32[260,1024]{1,0:T(8,128)}, f32[1024,1024]{1,0:T(8,128)}), (f32[260,1024]{1,0:T(8,128)}, f32[1024,1024]{1,0:T(8,128)})) %all-reduce.4.cloned.1.call-update) | async-done | bytes 5259280 | tf_op jit(solution)/shard_map/psum | solution.py:110
  347.7 2.3 slice.40
  350.0 1.5 fusion.39
  351.5 1.2 slice.44
  352.7 4.8 %copy.20 = f32[1024,1024]{1,0:T(8,128)} copy(f32[1024,1024]{1,0:T(8,128)} %get-tuple-element.32) | data formatting | bytes 8388608
  (19 shorter events, 0.1 us)
Async XLA Ops:
  7.2 60.7 %copy-start = (f32[256,1024]{1,0:T(8,128)S(1)}, f32[256,1024]{1,0:T(8,128)}, u32[]{:S(2)}) copy-start(f32[256,1024]{1,0:T(8,128)} %param.15) | copy-start | bytes 3145732
  7.2 147.8 %reduce-scatter.2.cloned.1.call-start = ((), (), s32[]{:S(2)}) async-start(), calls=%async_computation.1 | async-start | bytes 4792320 | tf_op jit(solution)/shard_map/reduce_scatter | solution.py:100
  67.2 2.4 copy-start.1
  67.2 280.5 %all-reduce.4.cloned.1.call-start = ((), (), s32[]{:S(2)}) async-start(), calls=%async_computation.2 | async-start | bytes 10551296 | tf_op jit(solution)/shard_map/psum | solution.py:110
  69.6 7.6 %copy-start.4 = (f32[1024]{0:T(1024)S(1)}, f32[1024]{0:T(1024)}, u32[]{:S(2)}) copy-start(f32[1024]{0:T(1024)} %param.19) | copy-start | bytes 12292
  69.6 7.6 %copy-start.5 = (f32[1024]{0:T(1024)S(1)}, f32[1024]{0:T(1024)}, u32[]{:S(2)}) copy-start(f32[1024]{0:T(1024)} %param.18) | copy-start | bytes 12292
  77.2 2.0 copy-start.6
  77.3 3.0 copy-start.2
  155.0 3.2 copy-start.8
  159.8 1.7 copy-start.7
  161.5 5.2 %copy-start.3 = (f32[1024,1024]{1,0:T(8,128)S(1)}, f32[1024,1024]{1,0:T(8,128)}, u32[]{:S(2)}) copy-start(f32[1024,1024]{1,0:T(8,128)} %param.17) | copy-start | bytes 12582916
Sparse Core Ops, SparseCore 0:
  67.3 87.6 reduce-scatter.1
  191.2 156.4 all-reduce.3
where the time goes:
time: 365 us; the launch traced here: 364 us
  waiting for transfers between devices  226 us (62%)
  Pallas kernels  53.2 us (15%)
  matrix products  48.2 us (13%)
  between operations  14.9 us (4%)
  local copies, waits for them, and re-layouts  14.4 us (4%)
  other arithmetic  7.36 us (2%)
    psum x1, waiting for transfers between devices, body(): head, g2 = lax.psum((head, grads[2]), ('path', 'trade'))  157 us
    reduce_scatter x1, waiting for transfers between devices, body(): mine = lax.psum_scatter(packed, 'trade', scatter_dimension=0, tiled=False)  69.6 us
    pallas_call x1, Pallas kernels, price(): pl.pallas_call(price_kernel, grid=(paths // tile,), in_specs=[pl.BlockSpe...  53.2 us
    dot_general x3, matrix products, twin_loss(): act_two = jnp.dot(hid_one, w_second, precision=highest) + b_second  19.7 us
    dot_general x3, matrix products, twin_loss(): jnp.dot(back_two, w_second.T, precision=highest) * jax.nn.sigmoid(act_one)  15.4 us
  transfers between devices with their start and end apart: 2, of which 2 were waited for; matrix products, arithmetic and copies ran while one was open for 5% of the time, Pallas kernels for 0%

commit v1 on v0

--- a/solution.py
+++ b/solution.py
@@ -54,14 +54,15 @@
     d_ref[...] = jnp.dot(w_scr[...], e_ref[...], preferred_element_type=jnp.float32)
 
 
-def price(factors, exposures, strikes, notionals, tile=256):
+def price(factors, exposures, strikes, notionals, half, halves, tile=256):
     paths, width = factors.shape
+    paths = paths // halves
     trades = exposures.shape[0]
     return pl.pallas_call(
         price_kernel,
         grid=(paths // tile,),
         in_specs=[
-            pl.BlockSpec((tile, width), lambda i: (i, 0)),
+            pl.BlockSpec((tile, width), lambda i: (i * halves + half, 0)),
             pl.BlockSpec((trades, width), lambda i: (0, 0)),
             pl.BlockSpec((1, trades), lambda i: (0, 0)),
             pl.BlockSpec((1, trades), lambda i: (0, 0)),
@@ -85,21 +86,22 @@
     factors, exposures, strikes, notionals, w_first, b_first, w_second, b_second, w_out, b_out
 ):
     paths, width = factors.shape
-    with jax.named_scope("price_trades"):
-        differential, value_parts = price(factors, exposures, strikes, notionals)
-    value = jnp.sum(value_parts, axis=1)
     groups = lax.axis_size("trade")
     own_rows = paths // groups
     first_row = lax.axis_index("trade") * own_rows
-    value_rows = -(-own_rows // width)
-    value_pad = jnp.pad(value.reshape(groups, own_rows), ((0, 0), (0, value_rows * width - own_rows)))
-    packed = jnp.concatenate(
-        [differential.reshape(groups, own_rows, width), value_pad.reshape(groups, value_rows, width)],
-        axis=1,
-    )
-    mine = lax.psum_scatter(packed, "trade", scatter_dimension=0, tiled=False)
-    my_diff = mine[:own_rows]
-    my_value = mine[own_rows:].reshape(-1)[:own_rows]
+    halves = 2
+    part_rows = own_rows // halves
+    diff_parts, value_parts = [], []
+    for half in range(halves):
+        with jax.named_scope("price_trades"):
+            diff_h, vpart_h = price(factors, exposures, strikes, notionals, half, halves)
+        value_h = jnp.sum(vpart_h, axis=1).reshape(groups, 1, part_rows)
+        packed = jnp.concatenate([diff_h.reshape(groups, part_rows, width), value_h], axis=1)
+        mine = lax.psum_scatter(packed, "trade", scatter_dimension=0, tiled=False)
+        diff_parts.append(mine[:part_rows])
+        value_parts.append(mine[part_rows])
+    my_diff = jnp.concatenate(diff_parts, axis=0)
+    my_value = jnp.concatenate(value_parts, axis=0)
     my_inputs = lax.dynamic_slice_in_dim(factors, first_row, own_rows, 0).astype(jnp.float32)
     scale = 1.0 / jnp.sqrt(jnp.float32(paths * lax.axis_size("path")))
     params = (w_first, b_first, w_second, b_second, w_out, b_out)

time: 365 us -> 415 us (1.14); the launches traced: 364 us -> 409 us
  waiting for transfers between devices: 226 us -> 263 us
    reduce_scatter x1 -> x2, waiting for transfers between devices: 69.6 us -> 106 us  [body(): mine = lax.psum_scatter(packed, 'trade', scatter_dimension=0, tiled=False)]
    pallas_call x1 -> x2, Pallas kernels: 53.2 us -> 55.3 us  [price(): pl.pallas_call(price_kernel, grid=(paths // tile,), in_specs=[pl.BlockSpe...]
  transfers between devices with their start and end apart: 2 -> 3, of which waited for: 2 -> 3; matrix products, arithmetic and copies ran while one was open for 5% -> 5% of each run, Pallas kernels for 0% -> 7%
where the time goes in v1:
time: 415 us; the launch traced here: 409 us
  waiting for transfers between devices  263 us (63%)
  Pallas kernels  55.3 us (13%)
  matrix products  48.1 us (12%)
  local copies, waits for them, and re-layouts  17.6 us (4%)
  between operations  15.1 us (4%)
  other arithmetic  10 us (2%)
    psum x1, waiting for transfers between devices, body(): head, g2 = lax.psum((head, grads[2]), ('path', 'trade'))  157 us
    reduce_scatter x2, waiting for transfers between devices, body(): mine = lax.psum_scatter(packed, 'trade', scatter_dimension=0, tiled=False)  106 us
    pallas_call x2, Pallas kernels, price(): pl.pallas_call(price_kernel, grid=(paths // tile,), in_specs=[pl.BlockSpe...  55.3 us
    dot_general x3, matrix products, twin_loss(): act_two = jnp.dot(hid_one, w_second, precision=highest) + b_second  19.7 us
    dot_general x3, matrix products, twin_loss(): jnp.dot(back_two, w_second.T, precision=highest) * jax.nn.sigmoid(act_one)  15.4 us
  transfers between devices with their start and end apart: 3, of which 3 were waited for; matrix products, arithmetic and copies ran while one was open for 5% of the time, Pallas kernels for 7%

profile of v1, /device:TPU:1, one launch (start us, length us, event | category | flops | bytes accessed | tf_op | source)
XLA Modules:
  0.0 408.9 jit_solution(1694388297787716458)
XLA Ops:
  7.2 27.7 %price_trades.3 = (f32[2048,256]{1,0:T(8,128)}, f32[2048,128]{1,0:T(8,128)}) custom-call(bf16[4096,256]{1,0:T(8,128)(2,1)} %f_ref.3, bf16[2048,256]{1,0:T(8,128)(2,1)} %e_ref.3, f32[1,2048]{1,0:T(1,128)} %bitcast.43, f32[1,2048]{1,0:T(1,128)} %bitcast.45), custom_call_target="tpu_custom_call" | custom-call | tf_op jit(solution)/shard_map/price_trades/pallas_call | solution.py:61
  34.9 1.6 reduce_sum.55
  36.5 3.1 pad_maximum_fusion.1
  39.7 27.6 %price_trades.2 = (f32[2048,256]{1,0:T(8,128)}, f32[2048,128]{1,0:T(8,128)}) custom-call(bf16[4096,256]{1,0:T(8,128)(2,1)} %f_ref.3, bf16[2048,256]{1,0:T(8,128)(2,1)} %e_ref.3, f32[1,2048]{1,0:T(1,128)} %bitcast.44, f32[1,2048]{1,0:T(1,128)} %bitcast.46), custom_call_target="tpu_custom_call" | custom-call | tf_op jit(solution)/shard_map/price_trades/pallas_call | solution.py:61
  67.3 1.6 reduce_sum.51
  68.8 3.1 pad_maximum_fusion
  72.7 1.7 fusion.28
  74.5 7.6 %fusion.24 = f32[512,1024]{1,0:T(8,128)S(1)} fusion(f32[1024,1024]{1,0:T(8,128)} %param.17, f32[512,1024]{1,0:T(8,128)S(1)} %fusion.28, f32[1024]{0:T(1024)S(1)} %copy-done.1), kind=kOutput, calls=%fused_computation.40 | convolution fusion | flops 3224895488 | bytes 8392704 | tf_op jit(solution)/shard_map/jvp()/dot_general | solution.py:14
  82.1 2.0 fusion.26
  84.1 1.0 copy-done.2
  85.1 5.1 %fusion.12 = f32[512,1024]{1,0:T(8,128)} fusion(f32[1024,1024]{1,0:T(8,128)S(1)} %copy-done.2, f32[1024]{0:T(1024)S(1)} %copy-done.4, f32[512,1024]{1,0:T(8,128)S(1)} %fusion.24, f32[1024]{0:T(1024)S(1)} %copy-done.5), kind=kOutput, calls=%fused_computation.26 | convolution fusion | flops 3223846912 | bytes 8396800 | tf_op jit(solution)/shard_map/jvp()/dot_general | solution.py:18
  90.2 27.8 %reduce-scatter.5.cloned.1.call-done = f32[1,257,256]{2,1,0:T(8,128)} async-done(((f32[8,257,256]{2,1,0:T(8,128)}), f32[1,257,256]{2,1,0:T(8,128)}) %reduce-scatter.5.cloned.1.call-update) | async-done | bytes 263184 | tf_op jit(solution)/shard_map/reduce_scatter | solution.py:100
  118.0 1.0 slice_bitcast_fusion
  119.0 78.2 %reduce-scatter.3.cloned.1.call-done = f32[1,257,256]{2,1,0:T(8,128)} async-done(((f32[8,257,256]{2,1,0:T(8,128)}), f32[1,257,256]{2,1,0:T(8,128)}) %reduce-scatter.3.cloned.1.call-update) | async-done | bytes 263184 | tf_op jit(solution)/shard_map/reduce_scatter | solution.py:100
  197.2 1.0 slice_bitcast_fusion.1
  198.2 3.1 fusion.15
  201.3 1.5 fusion.21
  202.8 1.0 fusion.44
  204.4 4.5 %fusion.10 = f32[1024,1024]{1,0:T(8,128)S(1)} fusion(f32[1024]{0:T(1024)S(1)} %copy-done.4, f32[512,1024]{1,0:T(8,128)S(1)} %fusion.44, f32[512,1024]{1,0:T(8,128)S(1)} %copy-done.7, f32[1024]{0:T(1024)S(1)} %copy-done.5, f32[512,1024]{1,0:T(8,128)S(1)} %fusion.28, f32[1024]{0:T(1024)S(1)} %copy-done.1), kind=kOutput, calls=%fused_computation.24 | convolution fusion | flops 3226468352 | bytes 10498048 | tf_op jit(solution)/shard_map/transpose(jvp())/dot_general | solution.py:18
  209.0 0.7 slice.54
  209.7 0.7 slice.53
  211.0 5.7 %fusion.40 = (f32[1024]{0:T(1024)S(1)}, f32[512,1024]{1,0:T(8,128)S(1)}, f32[1024]{0:T(1024)S(1)}) fusion(f32[512]{0:T(512)S(1)} %get-tuple-element.25, f32[512,1024]{1,0:T(8,128)S(1)} %copy-done.7, f32[1024]{0:T(1024)S(1)} %copy-done.5, f32[1024]{0:T(1024)S(1)} %copy-done.4, f32[1024,1024]{1,0:T(8,128)S(1)} %copy-done.3, f32[512,1024]{1,0:T(8,128)S(1)} %fusion.44, ...), kind=kOutput, calls=%fused_computation.58 | convolution fusion | flops 3236952064 | bytes 12605440 | tf_op jit(solution)/shard_map/transpose(jvp())/dot_general | solution.py:18
  216.7 5.3 %fusion.43 = (f32[1024]{0:T(1024)S(1)}, f32[512,1024]{1,0:T(8,128)S(1)}) fusion(f32[512,1024]{1,0:T(8,128)S(1)} %get-tuple-element.27, f32[1024,1024]{1,0:T(8,128)S(1)} %copy-done.3, f32[512,1024]{1,0:T(8,128)S(1)} %fusion.28, f32[1024]{0:T(1024)S(1)} %copy-done.1, f32[512,1024]{1,0:T(8,128)S(1)} %copy-done.8, f32[512,1024]{1,0:T(8,128)S(1)} %fusion.44), kind=kOutput, calls=%fused_computation.60 | convolution fusion | flops 3232758784 | bytes 14688256 | tf_op jit(solution)/shard_map/transpose(jvp())/dot_general | solution.py:14
  222.0 1.9 fusion.25
  224.6 6.8 %convolution_add_fusion = f32[1024,1024]{1,0:T(8,128)} fusion(f32[1024,1024]{1,0:T(8,128)S(1)} %fusion.10, f32[512,1024]{1,0:T(8,128)S(1)} %get-tuple-element.27, f32[512,1024]{1,0:T(8,128)S(1)} %fusion.28, f32[1024]{0:T(1024)S(1)} %copy-done.1), kind=kOutput, calls=%fused_computation.10 | convolution fusion | flops 3225944064 | bytes 12587008 | tf_op jit(solution)/shard_map/transpose(jvp())/dot_general | solution.py:14
  231.4 1.8 convolution_add_fusion.1
  233.2 2.2 concatenate.19
  235.4 156.8 %all-reduce.4.cloned.1.call-done = (f32[260,1024]{1,0:T(8,128)}, f32[1024,1024]{1,0:T(8,128)}) async-done(((f32[260,1024]{1,0:T(8,128)}, f32[1024,1024]{1,0:T(8,128)}), (f32[260,1024]{1,0:T(8,128)}, f32[1024,1024]{1,0:T(8,128)})) %all-reduce.4.cloned.1.call-update) | async-done | bytes 5259280 | tf_op jit(solution)/shard_map/psum | solution.py:112
  392.2 2.3 slice.55
  394.5 1.5 fusion.42
  396.0 1.2 slice.59
  397.2 4.8 %copy.19 = f32[1024,1024]{1,0:T(8,128)} copy(f32[1024,1024]{1,0:T(8,128)} %get-tuple-element.36) | data formatting | bytes 8388608
  (26 shorter events, 2.1 us)
Async XLA Ops:
  7.2 65.6 %copy-start = (f32[256,1024]{1,0:T(8,128)S(1)}, f32[256,1024]{1,0:T(8,128)}, u32[]{:S(2)}) copy-start(f32[256,1024]{1,0:T(8,128)} %param.15) | copy-start | bytes 3145732
  7.2 110.8 %reduce-scatter.5.cloned.1.call-start = ((), (), s32[]{:S(2)}) async-start(), calls=%async_computation.3 | async-start | bytes 2433024 | tf_op jit(solution)/shard_map/reduce_scatter | solution.py:100
  39.6 157.6 %reduce-scatter.3.cloned.1.call-start = ((), (), s32[]{:S(2)}) async-start(), calls=%async_computation.2 | async-start | bytes 2433024 | tf_op jit(solution)/shard_map/reduce_scatter | solution.py:100
  72.0 2.4 copy-start.1
  72.0 320.2 %all-reduce.4.cloned.1.call-start = ((), (), s32[]{:S(2)}) async-start(), calls=%async_computation.4 | async-start | bytes 10551296 | tf_op jit(solution)/shard_map/psum | solution.py:112
  74.4 7.7 %copy-start.4 = (f32[1024]{0:T(1024)S(1)}, f32[1024]{0:T(1024)}, u32[]{:S(2)}) copy-start(f32[1024]{0:T(1024)} %param.19) | copy-start | bytes 12292
  74.5 7.7 %copy-start.5 = (f32[1024]{0:T(1024)S(1)}, f32[1024]{0:T(1024)}, u32[]{:S(2)}) copy-start(f32[1024]{0:T(1024)} %param.18) | copy-start | bytes 12292
  82.1 2.0 copy-start.6
  82.1 3.0 copy-start.2
  198.1 3.2 copy-start.8
  202.8 1.6 copy-start.7
  204.4 6.6 %copy-start.3 = (f32[1024,1024]{1,0:T(8,128)S(1)}, f32[1024,1024]{1,0:T(8,128)}, u32[]{:S(2)}) copy-start(f32[1024,1024]{1,0:T(8,128)} %param.17) | copy-start | bytes 12582916
Sparse Core Ops, SparseCore 0:
  39.7 78.2 reduce-scatter.4
  121.7 75.3 reduce-scatter.2
  235.6 156.5 all-reduce.3

commit v2 on v1

--- a/solution.py
+++ b/solution.py
@@ -41,8 +41,7 @@
             notional = n_ref[:, cs]
             e = jnp.exp(-jnp.abs(m))
             soft = jnp.maximum(m, 0.0) + jnp.log1p(e)
-            rcp = 1.0 / (1.0 + e)
-            sig = jnp.where(m >= 0.0, rcp, e * rcp)
+            sig = jnp.exp(m - soft)
             w_scr[pl.ds(r, ROW_CHUNK), cs] = (sig * notional).astype(jnp.bfloat16)
             t = soft * notional
             for g in range(LANE_CHUNK // 128):
@@ -54,7 +53,7 @@
     d_ref[...] = jnp.dot(w_scr[...], e_ref[...], preferred_element_type=jnp.float32)
 
 
-def price(factors, exposures, strikes, notionals, half, halves, tile=256):
+def price(factors, exposures, strikes, notionals, half, halves, tile):
     paths, width = factors.shape
     paths = paths // halves
     trades = exposures.shape[0]
@@ -91,13 +90,25 @@
     first_row = lax.axis_index("trade") * own_rows
     halves = 2
     part_rows = own_rows // halves
+    me = lax.axis_index("trade")
+    z_len = groups // 2
     diff_parts, value_parts = [], []
     for half in range(halves):
         with jax.named_scope("price_trades"):
-            diff_h, vpart_h = price(factors, exposures, strikes, notionals, half, halves)
+            diff_h, vpart_h = price(factors, exposures, strikes, notionals, half, halves, part_rows)
         value_h = jnp.sum(vpart_h, axis=1).reshape(groups, 1, part_rows)
         packed = jnp.concatenate([diff_h.reshape(groups, part_rows, width), value_h], axis=1)
-        mine = lax.psum_scatter(packed, "trade", scatter_dimension=0, tiled=False)
+        mine = lax.dynamic_index_in_dim(packed, me, 0, keepdims=False)
+        for dy in range(2):
+            for dz in range(z_len):
+                if dy == 0 and dz == 0:
+                    continue
+
+                def dest(t, dy=dy, dz=dz):
+                    return ((t // z_len + dy) % 2) * z_len + (t % z_len + dz) % z_len
+
+                block = lax.dynamic_index_in_dim(packed, dest(me), 0, keepdims=False)
+                mine = mine + lax.ppermute(block, "trade", [(t, dest(t)) for t in range(groups)])
         diff_parts.append(mine[:part_rows])
         value_parts.append(mine[part_rows])
     my_diff = jnp.concatenate(diff_parts, axis=0)

time: 415 us -> 354 us (0.85)
  waiting for transfers between devices: 263 us -> 180 us
  starting transfers between devices: 0.12 us -> 26.2 us
    reduce_scatter x2 -> x0, waiting for transfers between devices: 106 us -> none  [body(): mine = lax.psum_scatter(packed, 'trade', scatter_dimension=0, tiled=False)]
    ppermute x0 -> x14, starting transfers between devices: none -> 26.1 us  [body(): lax.ppermute(block, 'trade', [(t, dest(t)) for t in range(groups)])]
    ppermute x0 -> x14, waiting for transfers between devices: none -> 25.6 us  [body(): lax.ppermute(block, 'trade', [(t, dest(t)) for t in range(groups)])]
    concatenate x2 -> x0, other arithmetic: 6.28 us -> none  [body(): jnp.concatenate([diff_h.reshape(groups, part_rows, width), value_h], axis=1)]
  transfers between devices with their start and end apart: 3 -> 15, of which waited for: 3 -> 5; matrix products, arithmetic and copies ran while one was open for 5% -> 7% of each run, Pallas kernels for 7% -> 8%
where the time goes in v2:
time: 354 us; the launch traced here: 348 us
  waiting for transfers between devices  180 us (51%)
  Pallas kernels  55.4 us (16%)
  matrix products  46.5 us (13%)
  starting transfers between devices  26.2 us (7%)
  between operations  15.5 us (4%)
  local copies, waits for them, and re-layouts  14.9 us (4%)
  other arithmetic  9.46 us (3%)
    psum x1, waiting for transfers between devices, body(): head, g2 = lax.psum((head, grads[2]), ('path', 'trade'))  154 us
    pallas_call x2, Pallas kernels, price(): pl.pallas_call(price_kernel, grid=(paths // tile,), in_specs=[pl.BlockSpe...  55.4 us
    ppermute x14, starting transfers between devices, body(): lax.ppermute(block, 'trade', [(t, dest(t)) for t in range(groups)])  26.1 us
    ppermute x14, waiting for transfers between devices, body(): lax.ppermute(block, 'trade', [(t, dest(t)) for t in range(groups)])  25.6 us
    dot_general x3, matrix products, twin_loss(): act_two = jnp.dot(hid_one, w_second, precision=highest) + b_second  20.5 us
    dot_general x3, matrix products, twin_loss(): jnp.dot(back_two, w_second.T, precision=highest) * jax.nn.sigmoid(act_one)  14.2 us
  transfers between devices with their start and end apart: 15, of which 5 were waited for; matrix products, arithmetic and copies ran while one was open for 7% of the time, Pallas kernels for 8%

profile of v2, /device:TPU:1, one launch (start us, length us, event | category | flops | bytes accessed | tf_op | source)
XLA Modules:
  0.0 348.1 jit_solution(17010306584984449361)
XLA Ops:
  7.3 27.8 %price_trades.3 = (f32[2048,256]{1,0:T(8,128)}, f32[2048,128]{1,0:T(8,128)}) custom-call(bf16[4096,256]{1,0:T(8,128)(2,1)} %f_ref.3, bf16[2048,256]{1,0:T(8,128)(2,1)} %e_ref.3, f32[1,2048]{1,0:T(1,128)} %bitcast.109, f32[1,2048]{1,0:T(1,128)} %bitcast.111), custom_call_target="tpu_custom_call" | custom-call | tf_op jit(solution)/shard_map/price_trades/pallas_call | solution.py:60
  35.1 1.7 reduce_sum.55
  36.8 1.7 fusion.25
  38.5 7.2 %collective-permute-start.13 = (f32[257,256]{1,0:T(8,128)}, f32[257,256]{1,0:T(8,128)S(1)}, u32[]{:S(2)}, u32[]{:S(2)}) collective-permute-start(f32[257,256]{1,0:T(8,128)} %fusion.25), channel_id=1, source_target_pairs={{0,7},{1,4},{2,5},{3,6},{4,3},{5,0},{6,1},{7,2},{8,15},{9,12},{10,... | collective-permute-start | bytes 789512 | tf_op jit(solution)/shard_map/ppermute | solution.py:111
  46.9 3.1 collective-permute-start.11
  50.2 2.3 collective-permute-start.9
  52.4 27.7 %price_trades.2 = (f32[2048,256]{1,0:T(8,128)}, f32[2048,128]{1,0:T(8,128)}) custom-call(bf16[4096,256]{1,0:T(8,128)(2,1)} %f_ref.3, bf16[2048,256]{1,0:T(8,128)(2,1)} %e_ref.3, f32[1,2048]{1,0:T(1,128)} %bitcast.110, f32[1,2048]{1,0:T(1,128)} %bitcast.112), custom_call_target="tpu_custom_call" | custom-call | tf_op jit(solution)/shard_map/price_trades/pallas_call | solution.py:60
  80.1 1.7 fusion.71
  81.9 8.2 %fusion.19 = f32[512,1024]{1,0:T(8,128)S(1)} fusion(f32[1024,1024]{1,0:T(8,128)} %param.17, f32[512,1024]{1,0:T(8,128)S(1)} %fusion.71, f32[1024]{0:T(1024)S(1)} %copy-done.10), kind=kOutput, calls=%fused_computation.64 | convolution fusion | flops 3224895488 | bytes 8392704 | tf_op jit(solution)/shard_map/jvp()/dot_general | solution.py:14
  90.1 3.9 %fusion.12 = f32[512,1024]{1,0:T(8,128)S(1)} fusion(f32[1024,1024]{1,0:T(8,128)S(1)} %copy-done.11, f32[1024]{0:T(1024)S(1)} %copy-done.13, f32[512,1024]{1,0:T(8,128)S(1)} %fusion.19, f32[1024]{0:T(1024)S(1)} %copy-done.14), kind=kOutput, calls=%fused_computation.40 | convolution fusion | flops 3223846912 | bytes 8396800 | tf_op jit(solution)/shard_map/jvp()/dot_general | solution.py:18
  95.3 2.2 fusion.91
  97.5 1.6 reduce_sum.51
  101.8 1.5 collective-permute-start.8
  103.4 5.3 %collective-permute-start.6 = (f32[257,256]{1,0:T(8,128)S(1)}, f32[257,256]{1,0:T(8,128)S(1)}, u32[]{:S(2)}, u32[]{:S(2)}) collective-permute-start(f32[257,256]{1,0:T(8,128)S(1)} %fusion.48), channel_id=1, source_target_pairs={{0,7},{1,4},{2,5},{3,6},{4,3},{5,0},{6,1},{7,2},{8,15},{9,12},{10,... | collective-permute-start | bytes 789512 | tf_op jit(solution)/shard_map/ppermute | solution.py:111
  109.1 2.0 fusion.21
  111.1 2.4 collective-permute-start.4
  114.5 14.1 %collective-permute-done.7 = f32[257,256]{1,0:T(8,128)S(1)} collective-permute-done((f32[257,256]{1,0:T(8,128)S(1)}, f32[257,256]{1,0:T(8,128)S(1)}, u32[]{:S(2)}, u32[]{:S(2)}) %collective-permute-start.7) | collective-permute-done | bytes 263200 | tf_op jit(solution)/shard_map/ppermute | solution.py:111
  128.6 1.9 collective-permute-start.1
  132.8 2.8 collective-permute-done.2
  135.7 1.6 collective-permute-done.1
  137.2 7.1 %collective-permute-done = f32[257,256]{1,0:T(8,128)S(1)} collective-permute-done((f32[257,256]{1,0:T(8,128)S(1)}, f32[257,256]{1,0:T(8,128)S(1)}, u32[]{:S(2)}, u32[]{:S(2)}) %collective-permute-start) | collective-permute-done | bytes 263200 | tf_op jit(solution)/shard_map/ppermute | solution.py:111
  144.6 1.5 fusion.75
  147.1 4.3 %fusion.10 = f32[1024,1024]{1,0:T(8,128)S(1)} fusion(f32[1024]{0:T(1024)S(1)} %copy-done.13, f32[512,1024]{1,0:T(8,128)S(1)} %fusion.73, f32[512,1024]{1,0:T(8,128)S(1)} %copy-done.16, f32[1024]{0:T(1024)S(1)} %copy-done.14, f32[512,1024]{1,0:T(8,128)S(1)} %copy-done.4, f32[1024]{0:T(1024)S(1)} %copy-done.10), kind=kOutput, calls=%fused_computation.38 | convolution fusion | flops 3226468352 | bytes 10498048 | tf_op jit(solution)/shard_map/transpose(jvp())/dot_general | solution.py:18
  152.1 6.0 %fusion.95 = (f32[1024]{0:T(1024)S(1)}, f32[512,1024]{1,0:T(8,128)S(1)}, f32[1024]{0:T(1024)S(1)}) fusion(f32[512]{0:T(512)S(1)} %get-tuple-element.25, f32[512,1024]{1,0:T(8,128)S(1)} %copy-done.16, f32[1024]{0:T(1024)S(1)} %copy-done.14, f32[1024]{0:T(1024)S(1)} %copy-done.13, f32[1024,1024]{1,0:T(8,128)S(1)} %copy-done.12, f32[512,1024]{1,0:T(8,128)S(1)} %fusion.73, ...), kind=kOutput, calls=%fused_computation.137 | convolution fusion | flops 3236952064 | bytes 12605440 | tf_op jit(solution)/shard_map/transpose(jvp())/dot_general | solution.py:18
  158.1 5.5 %fusion.98 = (f32[1024]{0:T(1024)S(1)}, f32[512,1024]{1,0:T(8,128)S(1)}) fusion(f32[512,1024]{1,0:T(8,128)S(1)} %get-tuple-element.27, f32[1024,1024]{1,0:T(8,128)S(1)} %copy-done.12, f32[512,1024]{1,0:T(8,128)S(1)} %copy-done.4, f32[1024]{0:T(1024)S(1)} %copy-done.10, f32[512,1024]{1,0:T(8,128)S(1)} %copy-done.18, f32[512,1024]{1,0:T(8,128)S(1)} %fusion.73), kind=kOutput, calls=%fused_computation.139 | convolution fusion | flops 3232758784 | bytes 14688256 | tf_op jit(solution)/shard_map/transpose(jvp())/dot_general | solution.py:14
  163.6 1.7 fusion.20
  166.0 6.8 %convolution_add_fusion = f32[1024,1024]{1,0:T(8,128)} fusion(f32[1024,1024]{1,0:T(8,128)S(1)} %fusion.10, f32[512,1024]{1,0:T(8,128)S(1)} %get-tuple-element.27, f32[512,1024]{1,0:T(8,128)S(1)} %copy-done.4, f32[1024]{0:T(1024)S(1)} %copy-done.10), kind=kOutput, calls=%fused_computation.24 | convolution fusion | flops 3225944064 | bytes 12587008 | tf_op jit(solution)/shard_map/transpose(jvp())/dot_general | solution.py:14
  172.8 1.8 convolution_add_fusion.1
  174.6 2.3 concatenate.19
  176.9 154.4 %all-reduce.4.cloned.1.call-done = (f32[260,1024]{1,0:T(8,128)}, f32[1024,1024]{1,0:T(8,128)}) async-done(((f32[260,1024]{1,0:T(8,128)}, f32[1024,1024]{1,0:T(8,128)}), (f32[260,1024]{1,0:T(8,128)}, f32[1024,1024]{1,0:T(8,128)})) %all-reduce.4.cloned.1.call-update) | async-done | bytes 5259280 | tf_op jit(solution)/shard_map/psum | solution.py:123
  331.3 2.3 slice.45
  336.3 4.8 %copy.19 = f32[1024,1024]{1,0:T(8,128)} copy(f32[1024,1024]{1,0:T(8,128)} %get-tuple-element.48) | data formatting | bytes 8388608
  (74 shorter events, 13.5 us)
Async XLA Ops:
  7.2 72.9 %copy-start = (f32[256,1024]{1,0:T(8,128)S(1)}, f32[256,1024]{1,0:T(8,128)}, u32[]{:S(2)}) copy-start(f32[256,1024]{1,0:T(8,128)} %param.15) | copy-start | bytes 3145732
  7.2 324.1 %all-reduce.4.cloned.1.call-start = ((), (), s32[]{:S(2)}) async-start(), calls=%async_computation | async-start | bytes 10551296 | tf_op jit(solution)/shard_map/psum | solution.py:123
  35.0 10.6 %copy-start.1 = (f32[2048,256]{1,0:T(8,128)S(1)}, f32[2048,256]{1,0:T(8,128)}, u32[]{:S(2)}) copy-start(f32[2048,256]{1,0:T(8,128)} %get-tuple-element.17) | copy-start | bytes 6291460
  38.5 62.6 %collective-permute-start.13 = (f32[257,256]{1,0:T(8,128)}, f32[257,256]{1,0:T(8,128)S(1)}, u32[]{:S(2)}, u32[]{:S(2)}) collective-permute-start(f32[257,256]{1,0:T(8,128)} %fusion.25), channel_id=1, source_target_pairs={{0,7},{1,4},{2,5},{3,6},{4,3},{5,0},{6,1},{7,2},{8,15},{9,12},{10,... | collective-permute-start | bytes 789512 | tf_op jit(solution)/shard_map/ppermute | solution.py:111
  46.9 56.5 %collective-permute-start.12 = (f32[257,256]{1,0:T(8,128)}, f32[257,256]{1,0:T(8,128)}, u32[]{:S(2)}, u32[]{:S(2)}) collective-permute-start(f32[257,256]{1,0:T(8,128)} %get-tuple-element.40), channel_id=1, source_target_pairs={{0,6},{1,7},{2,4},{3,5},{4,2},{5,3},{6,0},{7,1},{8,14},{9,15},{10,... | collective-permute-start | bytes 789512 | tf_op jit(solution)/shard_map/ppermute | solution.py:111
  46.9 56.5 %collective-permute-start.11 = (f32[257,256]{1,0:T(8,128)}, f32[257,256]{1,0:T(8,128)}, u32[]{:S(2)}, u32[]{:S(2)}) collective-permute-start(f32[257,256]{1,0:T(8,128)} %get-tuple-element.39), channel_id=1, source_target_pairs={{0,5},{1,6},{2,7},{3,4},{4,1},{5,2},{6,3},{7,0},{8,13},{9,14},{10,... | collective-permute-start | bytes 789512 | tf_op jit(solution)/shard_map/ppermute | solution.py:111
  50.0 58.7 %collective-permute-start.10 = (f32[257,256]{1,0:T(8,128)}, f32[257,256]{1,0:T(8,128)}, u32[]{:S(2)}, u32[]{:S(2)}) collective-permute-start(f32[257,256]{1,0:T(8,128)} %get-tuple-element.38), channel_id=1, source_target_pairs={{0,4},{1,5},{2,6},{3,7},{4,0},{5,1},{6,2},{7,3},{8,12},{9,13},{10,... | collective-permute-start | bytes 789512 | tf_op jit(solution)/shard_map/ppermute | solution.py:111
  50.2 60.9 %collective-permute-start.9 = (f32[257,256]{1,0:T(8,128)}, f32[257,256]{1,0:T(8,128)}, u32[]{:S(2)}, u32[]{:S(2)}) collective-permute-start(f32[257,256]{1,0:T(8,128)} %get-tuple-element.37), channel_id=1, source_target_pairs={{0,3},{1,0},{2,1},{3,2},{4,7},{5,4},{6,5},{7,6},{8,11},{9,8},{10,9... | collective-permute-start | bytes 789512 | tf_op jit(solution)/shard_map/ppermute | solution.py:111
  81.8 12.1 %copy-start.3 = (f32[512,1024]{1,0:T(8,128)}, f32[512,1024]{1,0:T(8,128)S(1)}, u32[]{:S(2)}) copy-start(f32[512,1024]{1,0:T(8,128)S(1)} %fusion.71) | copy-start | bytes 6291460
  81.8 8.2 %copy-start.11 = (f32[1024,1024]{1,0:T(8,128)S(1)}, f32[1024,1024]{1,0:T(8,128)}, u32[]{:S(2)}) copy-start(f32[1024,1024]{1,0:T(8,128)} %param.17) | copy-start | bytes 12582916
  81.9 8.2 %copy-start.13 = (f32[1024]{0:T(1024)S(1)}, f32[1024]{0:T(1024)}, u32[]{:S(2)}) copy-start(f32[1024]{0:T(1024)} %param.19) | copy-start | bytes 12292
  81.9 8.2 %copy-start.14 = (f32[1024]{0:T(1024)S(1)}, f32[1024]{0:T(1024)}, u32[]{:S(2)}) copy-start(f32[1024]{0:T(1024)} %param.18) | copy-start | bytes 12292
  90.1 3.9 %copy-start.15 = (f32[512,1024]{1,0:T(8,128)}, f32[512,1024]{1,0:T(8,128)S(1)}, u32[]{:S(2)}) copy-start(f32[512,1024]{1,0:T(8,128)S(1)} %fusion.19) | copy-start | bytes 6291460
  99.1 1.8 copy-start.2
  100.9 2.5 copy-start.8
  100.9 8.2 %copy-start.16 = (f32[512,1024]{1,0:T(8,128)S(1)}, f32[512,1024]{1,0:T(8,128)}, u32[]{:S(2)}) copy-start(f32[512,1024]{1,0:T(8,128)} %copy-done.15) | copy-start | bytes 6291460
  101.8 11.7 %collective-permute-start.8 = (f32[257,256]{1,0:T(8,128)S(1)}, f32[257,256]{1,0:T(8,128)S(1)}, u32[]{:S(2)}, u32[]{:S(2)}) collective-permute-start(f32[257,256]{1,0:T(8,128)S(1)} %copy-done.9), channel_id=1, source_target_pairs={{0,2},{1,3},{2,0},{3,1},{4,6},{5,7},{6,4},{7,5},{8,10},{9,11},{10,... | collective-permute-start | bytes 789512 | tf_op jit(solution)/shard_map/ppermute | solution.py:111
  103.4 25.2 %collective-permute-start.7 = (f32[257,256]{1,0:T(8,128)S(1)}, f32[257,256]{1,0:T(8,128)S(1)}, u32[]{:S(2)}, u32[]{:S(2)}) collective-permute-start(f32[257,256]{1,0:T(8,128)S(1)} %copy-done.8), channel_id=1, source_target_pairs={{0,1},{1,2},{2,3},{3,0},{4,5},{5,6},{6,7},{7,4},{8,9},{9,10},{10,1... | collective-permute-start | bytes 789512 | tf_op jit(solution)/shard_map/ppermute | solution.py:111
  103.4 25.2 %collective-permute-start.6 = (f32[257,256]{1,0:T(8,128)S(1)}, f32[257,256]{1,0:T(8,128)S(1)}, u32[]{:S(2)}, u32[]{:S(2)}) collective-permute-start(f32[257,256]{1,0:T(8,128)S(1)} %fusion.48), channel_id=1, source_target_pairs={{0,7},{1,4},{2,5},{3,6},{4,3},{5,0},{6,1},{7,2},{8,15},{9,12},{10,... | collective-permute-start | bytes 789512 | tf_op jit(solution)/shard_map/ppermute | solution.py:111
  108.7 21.9 %collective-permute-start.5 = (f32[257,256]{1,0:T(8,128)S(1)}, f32[257,256]{1,0:T(8,128)S(1)}, u32[]{:S(2)}, u32[]{:S(2)}) collective-permute-start(f32[257,256]{1,0:T(8,128)S(1)} %get-tuple-element.34), channel_id=1, source_target_pairs={{0,6},{1,7},{2,4},{3,5},{4,2},{5,3},{6,0},{7,1},{8,14},{9,15},{10,... | collective-permute-start | bytes 789512 | tf_op jit(solution)/shard_map/ppermute | solution.py:111
  111.1 21.7 %collective-permute-start.4 = (f32[257,256]{1,0:T(8,128)S(1)}, f32[257,256]{1,0:T(8,128)S(1)}, u32[]{:S(2)}, u32[]{:S(2)}) collective-permute-start(f32[257,256]{1,0:T(8,128)S(1)} %get-tuple-element.33), channel_id=1, source_target_pairs={{0,5},{1,6},{2,7},{3,4},{4,1},{5,2},{6,3},{7,0},{8,13},{9,14},{10,... | collective-permute-start | bytes 789512 | tf_op jit(solution)/shard_map/ppermute | solution.py:111
  113.5 19.3 %collective-permute-start.3 = (f32[257,256]{1,0:T(8,128)S(1)}, f32[257,256]{1,0:T(8,128)S(1)}, u32[]{:S(2)}, u32[]{:S(2)}) collective-permute-start(f32[257,256]{1,0:T(8,128)S(1)} %get-tuple-element.32), channel_id=1, source_target_pairs={{0,4},{1,5},{2,6},{3,7},{4,0},{5,1},{6,2},{7,3},{8,12},{9,13},{10,... | collective-permute-start | bytes 789512 | tf_op jit(solution)/shard_map/ppermute | solution.py:111
  128.6 7.1 %collective-permute-start.2 = (f32[257,256]{1,0:T(8,128)S(1)}, f32[257,256]{1,0:T(8,128)S(1)}, u32[]{:S(2)}, u32[]{:S(2)}) collective-permute-start(f32[257,256]{1,0:T(8,128)S(1)} %get-tuple-element.31), channel_id=1, source_target_pairs={{0,3},{1,0},{2,1},{3,2},{4,7},{5,4},{6,5},{7,6},{8,11},{9,8},{10,9... | collective-permute-start | bytes 789512 | tf_op jit(solution)/shard_map/ppermute | solution.py:111
  128.6 8.6 %collective-permute-start.1 = (f32[257,256]{1,0:T(8,128)S(1)}, f32[257,256]{1,0:T(8,128)S(1)}, u32[]{:S(2)}, u32[]{:S(2)}) collective-permute-start(f32[257,256]{1,0:T(8,128)S(1)} %get-tuple-element.30), channel_id=1, source_target_pairs={{0,2},{1,3},{2,0},{3,1},{4,6},{5,7},{6,4},{7,5},{8,10},{9,11},{10,... | collective-permute-start | bytes 789512 | tf_op jit(solution)/shard_map/ppermute | solution.py:111
  130.6 13.8 %collective-permute-start = (f32[257,256]{1,0:T(8,128)S(1)}, f32[257,256]{1,0:T(8,128)S(1)}, u32[]{:S(2)}, u32[]{:S(2)}) collective-permute-start(f32[257,256]{1,0:T(8,128)S(1)} %get-tuple-element.29), channel_id=1, source_target_pairs={{0,1},{1,2},{2,3},{3,0},{4,5},{5,6},{6,7},{7,4},{8,9},{9,10},{10,1... | collective-permute-start | bytes 789512 | tf_op jit(solution)/shard_map/ppermute | solution.py:111
  132.8 11.7 %copy-start.6 = (f32[257,256]{1,0:T(8,128)}, f32[257,256]{1,0:T(8,128)S(1)}, u32[]{:S(2)}) copy-start(f32[257,256]{1,0:T(8,128)S(1)} %fusion.34) | copy-start | bytes 789508
  132.8 11.8 %copy-start.4 = (f32[512,1024]{1,0:T(8,128)S(1)}, f32[512,1024]{1,0:T(8,128)}, u32[]{:S(2)}) copy-start(f32[512,1024]{1,0:T(8,128)} %copy-done.3) | copy-start | bytes 6291460
  132.8 11.8 %copy-start.7 = (f32[512,256]{1,0:T(8,128)S(1)}, f32[512,256]{1,0:T(8,128)}, u32[]{:S(2)}) copy-start(f32[512,256]{1,0:T(8,128)} %fusion.91) | copy-start | bytes 1572868
  132.8 11.8 %copy-start.18 = (f32[512,1024]{1,0:T(8,128)S(1)}, f32[512,1024]{1,0:T(8,128)}, u32[]{:S(2)}) copy-start(f32[512,1024]{1,0:T(8,128)} %copy-done.17) | copy-start | bytes 6291460
  147.1 4.3 %slice-start = ((f32[257,256]{1,0:T(8,128)}), f32[1,256]{1,0:T(1,128)S(1)}, s32[]{:S(2)}) async-start(f32[257,256]{1,0:T(8,128)} %copy-done.5), calls=%async_computation.1 | async-start | bytes 2048 | tf_op jit(solution)/shard_map/slice | solution.py:113
  147.1 4.3 %slice-start.1 = ((f32[257,256]{1,0:T(8,128)}), f32[1,256]{1,0:T(1,128)S(1)}, s32[]{:S(2)}) async-start(f32[257,256]{1,0:T(8,128)} %copy-done.6), calls=%async_computation.2 | async-start | bytes 2048 | tf_op jit(solution)/shard_map/slice | solution.py:113
  147.1 4.9 %copy-start.12 = (f32[1024,1024]{1,0:T(8,128)S(1)}, f32[1024,1024]{1,0:T(8,128)}, u32[]{:S(2)}) copy-start(f32[1024,1024]{1,0:T(8,128)} %param.17) | copy-start | bytes 12582916
  (4 other events, 5.6 us)
Sparse Core Ops, SparseCore 0:
  177.0 154.2 all-reduce.3
